TPU v7x, 512 devices: a whole 4x8x8 slice. The times are simulated.
512 devices in a mesh: param: 32 (over x, z), ex: 16 (over y, core).
Axes of the slice: x: 4, y: 8, z: 8, core: 2. Of those that a mesh axis runs over, the one named last changes fastest.
Arguments:
- adapter_gradients: bfloat16 [512, 131072], P('ex', 'param'), may hold values from -560 to 560
- sign_hash_keys: int32 [4], replicated, may hold values from 1 to 16777215
- target_indices: int32 [256], replicated, may hold values from 0 to 511
Outputs:
- features: float32 [512, 8192], P('ex', 'param')
- scores: float32 [512, 256], P('ex')
All inputs are finite; a program needn't handle non-finite values.
Results may differ from a plain program's by a relative error of at most 0.0003.
Values sent between devices are 32-bit elements; how exact they have to be, the bound alone decides.
No kernel may reach another device: no remote copies, remote signals or barrier semaphores. Data moves between devices by JAX's collectives and lax.ppermute only.
A program may use at most 128 MiB of HBM per device.

v0:
```python
import jax
import jax.numpy as jnp
from jax import lax
from jax.sharding import PartitionSpec as P

K = 8192


norm_eps = 1e-06


def sign_block(sign_hash_keys, first_row, row_count, col_count):
    mult_row = sign_hash_keys[0] | 1
    mult_col = sign_hash_keys[1] | 1
    seed_add = sign_hash_keys[2]
    mix_mult = sign_hash_keys[3] | 1
    row_ids = first_row + lax.iota(jnp.int32, row_count)[:, None]
    col_ids = lax.iota(jnp.int32, col_count)[None, :]
    hashed = row_ids * mult_row + col_ids * mult_col + seed_add
    hashed = hashed ^ lax.shift_right_logical(hashed, jnp.full_like(hashed, 16))
    hashed = hashed * mix_mult
    hashed = hashed ^ lax.shift_right_logical(hashed, jnp.full_like(hashed, 13))
    hashed = hashed * jnp.int32(-1028477387)
    hashed = hashed ^ lax.shift_right_logical(hashed, jnp.full_like(hashed, 16))
    return jnp.where(hashed < 0, 1.0, -1.0).astype(jnp.bfloat16)


def local(adapter_gradients, sign_hash_keys, target_indices):
    resident_example, resident_rows = adapter_gradients.shape
    row_base = lax.axis_index("param") * jnp.int32(resident_rows)
    turn_count = 8
    rows_per_tile = resident_rows // turn_count
    scale_k = jnp.float32(K)

    def accumulate(tile_idx, totals):
        start_offset = tile_idx * jnp.int32(rows_per_tile)
        gradient_slab = lax.dynamic_slice_in_dim(adapter_gradients, start_offset, rows_per_tile, 1)
        signs = sign_block(sign_hash_keys, row_base + start_offset, rows_per_tile, K)
        return totals + jnp.dot(gradient_slab, signs, preferred_element_type=jnp.float32)

    partial_sums = lax.fori_loop(
        jnp.int32(0),
        jnp.int32(turn_count),
        accumulate,
        jnp.zeros((resident_example, K), jnp.float32),
    )
    projected = lax.psum_scatter(partial_sums, "param", scatter_dimension=1, tiled=True)
    own_squares = jnp.sum(projected * projected, axis=1)
    total_sq = lax.psum(own_squares, "param")
    features = projected * jnp.sqrt(scale_k / (total_sq + norm_eps))[:, None]
    pool_rows = lax.all_gather(features, "ex", axis=0, tiled=True)
    targets = jnp.take(pool_rows, target_indices, axis=0)
    partial_dots = jnp.dot(features, targets.T, precision=lax.Precision.HIGHEST)
    scores = lax.psum(partial_dots, "param") / scale_k
    return (features, scores)


def solution(mesh):
    return jax.shard_map(
        local,
        mesh=mesh,
        in_specs=(P("ex", "param"), P(), P()),
        out_specs=(P("ex", "param"), P("ex", None)),
        check_vma=False,
    )
```

profile of v0, /device:TPU:8, one launch (start us, length us, event | category | flops | bytes accessed | tf_op | source)
XLA Modules:
  0.0 555.2 jit_solution(16775991105922428957)
XLA Ops:
  7.2 1.4 fusion.24
  10.4 81.0 %while.12 = (s32[]{:T(128)}, f32[32,8192]{1,0:T(8,128)S(1)}, bf16[32,4096]{1,0:T(8,128)(2,1)}, s32[]{:T(128)}, s32[]{:T(128)}, /*index=5*/s32[]{:T(128)}, s32[4]...) while((s32[]{:T(128)}, f32[32,8192]{1,0:T(8,128)S(1)}, ...), condition=%wide.region_1.2_spmd.clone, body=%wide.region_0.1_spmd.clone.sunk | while | flops 323494912 | bytes 2200785 | solution.py:41
  10.5 1.3 slice.29
  11.8 8.8 %convolution_add_fusion.2 = f32[32,8192]{1,0:T(8,128)S(1)} fusion(s32[]{:T(128)} %get-tuple-element.187, s32[]{:T(128)} %bitcast.6, s32[8192]{0:T(1024)S(1)} %iota_multiply_fusion.2, s32[512]{0:T(512)S(1)} %add_multiply_fusion.2, f32[32,8192]{1,0:T(8,128)S(1)} %get-tuple-element.169, pred[]{:T(512)S(6)} %compare.3, ...), kind=kOutput, calls=%fused_computation.8.clone.1 | convolution fusion | flops 323485696 | bytes 2165765 | tf_op jit(solution)/shard_map/while/body/dot_general | solution.py:39
  20.6 1.3 slice.29
  21.9 8.8 %convolution_add_fusion.2 = f32[32,8192]{1,0:T(8,128)S(1)} fusion(s32[]{:T(128)} %get-tuple-element.187, s32[]{:T(128)} %bitcast.6, s32[8192]{0:T(1024)S(1)} %iota_multiply_fusion.2, s32[512]{0:T(512)S(1)} %add_multiply_fusion.2, f32[32,8192]{1,0:T(8,128)S(1)} %get-tuple-element.169, pred[]{:T(512)S(6)} %compare.3, ...), kind=kOutput, calls=%fused_computation.8.clone.1 | convolution fusion | flops 323485696 | bytes 2165765 | tf_op jit(solution)/shard_map/while/body/dot_general | solution.py:39
  30.8 1.3 slice.29
  32.1 8.8 %convolution_add_fusion.2 = f32[32,8192]{1,0:T(8,128)S(1)} fusion(s32[]{:T(128)} %get-tuple-element.187, s32[]{:T(128)} %bitcast.6, s32[8192]{0:T(1024)S(1)} %iota_multiply_fusion.2, s32[512]{0:T(512)S(1)} %add_multiply_fusion.2, f32[32,8192]{1,0:T(8,128)S(1)} %get-tuple-element.169, pred[]{:T(512)S(6)} %compare.3, ...), kind=kOutput, calls=%fused_computation.8.clone.1 | convolution fusion | flops 323485696 | bytes 2165765 | tf_op jit(solution)/shard_map/while/body/dot_general | solution.py:39
  40.9 1.3 slice.29
  42.2 8.8 %convolution_add_fusion.2 = f32[32,8192]{1,0:T(8,128)S(1)} fusion(s32[]{:T(128)} %get-tuple-element.187, s32[]{:T(128)} %bitcast.6, s32[8192]{0:T(1024)S(1)} %iota_multiply_fusion.2, s32[512]{0:T(512)S(1)} %add_multiply_fusion.2, f32[32,8192]{1,0:T(8,128)S(1)} %get-tuple-element.169, pred[]{:T(512)S(6)} %compare.3, ...), kind=kOutput, calls=%fused_computation.8.clone.1 | convolution fusion | flops 323485696 | bytes 2165765 | tf_op jit(solution)/shard_map/while/body/dot_general | solution.py:39
  51.0 1.3 slice.29
  52.3 8.8 %convolution_add_fusion.2 = f32[32,8192]{1,0:T(8,128)S(1)} fusion(s32[]{:T(128)} %get-tuple-element.187, s32[]{:T(128)} %bitcast.6, s32[8192]{0:T(1024)S(1)} %iota_multiply_fusion.2, s32[512]{0:T(512)S(1)} %add_multiply_fusion.2, f32[32,8192]{1,0:T(8,128)S(1)} %get-tuple-element.169, pred[]{:T(512)S(6)} %compare.3, ...), kind=kOutput, calls=%fused_computation.8.clone.1 | convolution fusion | flops 323485696 | bytes 2165765 | tf_op jit(solution)/shard_map/while/body/dot_general | solution.py:39
  61.1 1.3 slice.29
  62.4 8.8 %convolution_add_fusion.2 = f32[32,8192]{1,0:T(8,128)S(1)} fusion(s32[]{:T(128)} %get-tuple-element.187, s32[]{:T(128)} %bitcast.6, s32[8192]{0:T(1024)S(1)} %iota_multiply_fusion.2, s32[512]{0:T(512)S(1)} %add_multiply_fusion.2, f32[32,8192]{1,0:T(8,128)S(1)} %get-tuple-element.169, pred[]{:T(512)S(6)} %compare.3, ...), kind=kOutput, calls=%fused_computation.8.clone.1 | convolution fusion | flops 323485696 | bytes 2165765 | tf_op jit(solution)/shard_map/while/body/dot_general | solution.py:39
  71.3 1.3 slice.29
  72.6 8.8 %convolution_add_fusion.2 = f32[32,8192]{1,0:T(8,128)S(1)} fusion(s32[]{:T(128)} %get-tuple-element.187, s32[]{:T(128)} %bitcast.6, s32[8192]{0:T(1024)S(1)} %iota_multiply_fusion.2, s32[512]{0:T(512)S(1)} %add_multiply_fusion.2, f32[32,8192]{1,0:T(8,128)S(1)} %get-tuple-element.169, pred[]{:T(512)S(6)} %compare.3, ...), kind=kOutput, calls=%fused_computation.8.clone.1 | convolution fusion | flops 323485696 | bytes 2165765 | tf_op jit(solution)/shard_map/while/body/dot_general | solution.py:39
  81.4 1.3 slice.29
  82.7 8.8 %convolution_add_fusion.2 = f32[32,8192]{1,0:T(8,128)S(1)} fusion(s32[]{:T(128)} %get-tuple-element.187, s32[]{:T(128)} %bitcast.6, s32[8192]{0:T(1024)S(1)} %iota_multiply_fusion.2, s32[512]{0:T(512)S(1)} %add_multiply_fusion.2, f32[32,8192]{1,0:T(8,128)S(1)} %get-tuple-element.169, pred[]{:T(512)S(6)} %compare.3, ...), kind=kOutput, calls=%fused_computation.8.clone.1 | convolution fusion | flops 323485696 | bytes 2165765 | tf_op jit(solution)/shard_map/while/body/dot_general | solution.py:39
  91.5 1.0 copy-done
  92.5 225.0 %reduce-scatter.2.cloned.1.call-done = f32[32,256]{1,0:T(8,128)} async-done(((f32[32,8192]{1,0:T(8,128)}), f32[32,256]{1,0:T(8,128)}) %reduce-scatter.2.cloned.1.call-update) | async-done | bytes 32784 | tf_op jit(solution)/shard_map/reduce_scatter | solution.py:47
  318.4 72.3 %psum.14 = f32[32]{0:T(128)S(1)} all-reduce(f32[32]{0:T(128)S(1)} %multiply_reduce_fusion), channel_id=1, replica_groups=mesh['param'=32,'ex'=16] {'param'}, use_global_device_ids=true, to_apply=%region_4.5 | all-reduce | flops 32 | bytes 256 | tf_op jit(solution)/shard_map/psum | solution.py:49
  391.5 17.1 %all_gather.3 = f32[512,256]{1,0:T(8,128)S(1)} all-gather(f32[32,256]{1,0:T(8,128)S(1)} %broadcast_multiply_fusion.1), channel_id=1, replica_groups=mesh['param'=32,'ex'=16] {'ex'}, dimensions={0}, use_global_device_ids=true | all-gather | bytes 557056 | tf_op jit(solution)/shard_map/all_gather | solution.py:51
  408.7 1.0 gather_fusion
  410.1 137.7 %psum.15 = f32[32,256]{1,0:T(8,128)S(1)} all-reduce(f32[32,256]{1,0:T(8,128)S(1)} %fusion.19), channel_id=1, replica_groups=mesh['param'=32,'ex'=16] {'param'}, use_global_device_ids=true, to_apply=%region_5.6 | all-reduce | flops 8192 | bytes 65536 | tf_op jit(solution)/shard_map/psum | solution.py:54
  (32 shorter events, 3.0 us)
Async XLA Ops:
  7.2 310.4 %reduce-scatter.2.cloned.1.call-start = ((), (), s32[]{:S(2)}) async-start(), calls=%async_computation.1 | async-start | bytes 1081344 | tf_op jit(solution)/shard_map/reduce_scatter | solution.py:47
  91.5 1.0 copy-start
  91.5 1.0 copy-start.2
  391.5 18.1 %copy-start.1 = (f32[32,256]{1,0:T(8,128)}, f32[32,256]{1,0:T(8,128)S(1)}, u32[]{:S(2)}) copy-start(f32[32,256]{1,0:T(8,128)S(1)} %broadcast_multiply_fusion.1) | copy-start | bytes 98308
Sparse Core Ops, SparseCore 0:
  92.6 224.9 reduce-scatter.1
where the time goes:
time: 556 us; the launch traced here: 555 us
  blocking collectives  227 us (41%)
  waiting for transfers between devices  225 us (40%)
  matrix products  70.5 us (13%)
  between operations  16 us (3%)
  local copies, waits for them, and re-layouts  13.7 us (2%)
    reduce_scatter x1, waiting for transfers between devices, local(): lax.psum_scatter(partial_sums, 'param', scatter_dimension=1, tiled=True)  225 us
    psum x1, blocking collectives, local(): scores = lax.psum(partial_dots, 'param') / scale_k  138 us
    psum x1, blocking collectives, local(): total_sq = lax.psum(own_squares, 'param')  72.3 us
    dot_general x8, matrix products, accumulate(): jnp.dot(gradient_slab, signs, preferred_element_type=jnp.float32)  70 us
    all_gather x1, blocking collectives, local(): pool_rows = lax.all_gather(features, 'ex', axis=0, tiled=True)  17.1 us
  transfers between devices with their start and end apart: 1, of which 1 were waited for; matrix products, arithmetic and copies ran while one was open for 0% of the time, Pallas kernels for 0%

commit v1 on v0

--- a/solution.py
+++ b/solution.py
@@ -25,6 +25,15 @@
     return jnp.where(hashed < 0, 1.0, -1.0).astype(jnp.bfloat16)
 
 
+def butterfly_sum(values, axis, count):
+    distance = 1
+    while distance < count:
+        pairs = [(j, j ^ distance) for j in range(count)]
+        values = values + lax.ppermute(values, axis, pairs)
+        distance *= 2
+    return values
+
+
 def local(adapter_gradients, sign_hash_keys, target_indices):
     resident_example, resident_rows = adapter_gradients.shape
     row_base = lax.axis_index("param") * jnp.int32(resident_rows)
@@ -44,14 +53,26 @@
         accumulate,
         jnp.zeros((resident_example, K), jnp.float32),
     )
-    projected = lax.psum_scatter(partial_sums, "param", scatter_dimension=1, tiled=True)
+    param_count = lax.psum(1, "param")
+    col_width = K // param_count
+    blocks = partial_sums.reshape(resident_example, param_count, col_width)
+    blocks = lax.all_to_all(blocks, "param", 1, 1, tiled=True)
+    projected = jnp.sum(blocks, axis=1)
+    pool_rows = lax.all_gather(projected, "ex", axis=0, tiled=True)
+    target_rows = jnp.take(pool_rows, target_indices, axis=0)
+    partial_dots = jnp.dot(projected, target_rows.T, precision=lax.Precision.HIGHEST)
     own_squares = jnp.sum(projected * projected, axis=1)
-    total_sq = lax.psum(own_squares, "param")
-    features = projected * jnp.sqrt(scale_k / (total_sq + norm_eps))[:, None]
-    pool_rows = lax.all_gather(features, "ex", axis=0, tiled=True)
-    targets = jnp.take(pool_rows, target_indices, axis=0)
-    partial_dots = jnp.dot(features, targets.T, precision=lax.Precision.HIGHEST)
-    scores = lax.psum(partial_dots, "param") / scale_k
+    target_squares = jnp.sum(target_rows * target_rows, axis=1)
+    packed = jnp.concatenate([partial_dots.reshape(-1), own_squares, target_squares])
+    packed = butterfly_sum(packed, "param", param_count)
+    dot_count = partial_dots.size
+    dots = packed[:dot_count].reshape(partial_dots.shape)
+    total_sq = packed[dot_count:dot_count + resident_example]
+    target_sq = packed[dot_count + resident_example:]
+    own_scale = jnp.sqrt(scale_k / (total_sq + norm_eps))
+    target_scale = jnp.sqrt(scale_k / (target_sq + norm_eps))
+    features = projected * own_scale[:, None]
+    scores = dots * own_scale[:, None] * target_scale[None, :] / scale_k
     return (features, scores)
 
 

time: 556 us -> 185 us (0.33)
  the two profiles are of different devices: /device:TPU:8 before, /device:TPU:64 now
where the time goes in v1:
time: 185 us; the launch traced here: 183 us
  matrix products  69.9 us (38%)
  waiting for transfers between devices  50 us (27%)
  starting transfers between devices  26.7 us (14%)
  blocking collectives  19 us (10%)
  local copies, waits for them, and re-layouts  13.4 us (7%)
  between operations  2.69 us (1%)
    dot_general x8, matrix products, accumulate(): jnp.dot(gradient_slab, signs, preferred_element_type=jnp.float32)  69.5 us
    all_to_all x1, waiting for transfers between devices, local(): blocks = lax.all_to_all(blocks, 'param', 1, 1, tiled=True)  28.5 us
    ppermute x5, waiting for transfers between devices, butterfly_sum(): values = values + lax.ppermute(values, axis, pairs)  21.5 us
    all_gather x1, blocking collectives, local(): pool_rows = lax.all_gather(projected, 'ex', axis=0, tiled=True)  19 us
    ppermute x5, starting transfers between devices, butterfly_sum(): values = values + lax.ppermute(values, axis, pairs)  14 us
    all_to_all x1, starting transfers between devices, local(): blocks = lax.all_to_all(blocks, 'param', 1, 1, tiled=True)  12.7 us
    slice x8, local copies, waits for them, and re-layouts, sign_block(): seed_add = sign_hash_keys[2]  9.85 us
  transfers between devices with their start and end apart: 6, of which 6 were waited for; matrix products, arithmetic and copies ran while one was open for 0% of the time, Pallas kernels for 0%

profile of v1, /device:TPU:64, one launch (start us, length us, event | category | flops | bytes accessed | tf_op | source)
XLA Modules:
  0.0 183.4 jit_solution(9856501496791513573)
XLA Ops:
  0.6 1.4 fusion.27
  3.9 79.9 %while.12 = (s32[]{:T(128)}, f32[32,8192]{1,0:T(8,128)S(1)}, bf16[32,4096]{1,0:T(8,128)(2,1)}, s32[]{:T(128)}, s32[]{:T(128)}, /*index=5*/s32[]{:T(128)}, s32[4]...) while((s32[]{:T(128)}, f32[32,8192]{1,0:T(8,128)S(1)}, ...), condition=%wide.region_1.2_spmd.clone, body=%wide.region_0.1_spmd.clone.sunk | while | flops 323494912 | bytes 2200785 | solution.py:50
  4.0 1.2 slice.54
  5.2 8.7 %convolution_add_fusion.2 = f32[32,8192]{1,0:T(8,128)S(1)} fusion(s32[]{:T(128)} %get-tuple-element.189, s32[]{:T(128)} %bitcast.13, s32[8192]{0:T(1024)S(1)} %iota_multiply_fusion.2, s32[512]{0:T(512)S(1)} %add_multiply_fusion.2, f32[32,8192]{1,0:T(8,128)S(1)} %get-tuple-element.171, pred[]{:T(512)S(6)} %compare.3, ...), kind=kOutput, calls=%fused_computation.8.clone.1 | convolution fusion | flops 323485696 | bytes 2165765 | tf_op jit(solution)/shard_map/while/body/dot_general | solution.py:48
  15.2 8.7 %convolution_add_fusion.2 = f32[32,8192]{1,0:T(8,128)S(1)} fusion(s32[]{:T(128)} %get-tuple-element.189, s32[]{:T(128)} %bitcast.13, s32[8192]{0:T(1024)S(1)} %iota_multiply_fusion.2, s32[512]{0:T(512)S(1)} %add_multiply_fusion.2, f32[32,8192]{1,0:T(8,128)S(1)} %get-tuple-element.171, pred[]{:T(512)S(6)} %compare.3, ...), kind=kOutput, calls=%fused_computation.8.clone.1 | convolution fusion | flops 323485696 | bytes 2165765 | tf_op jit(solution)/shard_map/while/body/dot_general | solution.py:48
  25.2 8.7 %convolution_add_fusion.2 = f32[32,8192]{1,0:T(8,128)S(1)} fusion(s32[]{:T(128)} %get-tuple-element.189, s32[]{:T(128)} %bitcast.13, s32[8192]{0:T(1024)S(1)} %iota_multiply_fusion.2, s32[512]{0:T(512)S(1)} %add_multiply_fusion.2, f32[32,8192]{1,0:T(8,128)S(1)} %get-tuple-element.171, pred[]{:T(512)S(6)} %compare.3, ...), kind=kOutput, calls=%fused_computation.8.clone.1 | convolution fusion | flops 323485696 | bytes 2165765 | tf_op jit(solution)/shard_map/while/body/dot_general | solution.py:48
  35.2 8.7 %convolution_add_fusion.2 = f32[32,8192]{1,0:T(8,128)S(1)} fusion(s32[]{:T(128)} %get-tuple-element.189, s32[]{:T(128)} %bitcast.13, s32[8192]{0:T(1024)S(1)} %iota_multiply_fusion.2, s32[512]{0:T(512)S(1)} %add_multiply_fusion.2, f32[32,8192]{1,0:T(8,128)S(1)} %get-tuple-element.171, pred[]{:T(512)S(6)} %compare.3, ...), kind=kOutput, calls=%fused_computation.8.clone.1 | convolution fusion | flops 323485696 | bytes 2165765 | tf_op jit(solution)/shard_map/while/body/dot_general | solution.py:48
  45.2 8.7 %convolution_add_fusion.2 = f32[32,8192]{1,0:T(8,128)S(1)} fusion(s32[]{:T(128)} %get-tuple-element.189, s32[]{:T(128)} %bitcast.13, s32[8192]{0:T(1024)S(1)} %iota_multiply_fusion.2, s32[512]{0:T(512)S(1)} %add_multiply_fusion.2, f32[32,8192]{1,0:T(8,128)S(1)} %get-tuple-element.171, pred[]{:T(512)S(6)} %compare.3, ...), kind=kOutput, calls=%fused_computation.8.clone.1 | convolution fusion | flops 323485696 | bytes 2165765 | tf_op jit(solution)/shard_map/while/body/dot_general | solution.py:48
  55.1 8.7 %convolution_add_fusion.2 = f32[32,8192]{1,0:T(8,128)S(1)} fusion(s32[]{:T(128)} %get-tuple-element.189, s32[]{:T(128)} %bitcast.13, s32[8192]{0:T(1024)S(1)} %iota_multiply_fusion.2, s32[512]{0:T(512)S(1)} %add_multiply_fusion.2, f32[32,8192]{1,0:T(8,128)S(1)} %get-tuple-element.171, pred[]{:T(512)S(6)} %compare.3, ...), kind=kOutput, calls=%fused_computation.8.clone.1 | convolution fusion | flops 323485696 | bytes 2165765 | tf_op jit(solution)/shard_map/while/body/dot_general | solution.py:48
  65.1 8.7 %convolution_add_fusion.2 = f32[32,8192]{1,0:T(8,128)S(1)} fusion(s32[]{:T(128)} %get-tuple-element.189, s32[]{:T(128)} %bitcast.13, s32[8192]{0:T(1024)S(1)} %iota_multiply_fusion.2, s32[512]{0:T(512)S(1)} %add_multiply_fusion.2, f32[32,8192]{1,0:T(8,128)S(1)} %get-tuple-element.171, pred[]{:T(512)S(6)} %compare.3, ...), kind=kOutput, calls=%fused_computation.8.clone.1 | convolution fusion | flops 323485696 | bytes 2165765 | tf_op jit(solution)/shard_map/while/body/dot_general | solution.py:48
  75.1 8.7 %convolution_add_fusion.2 = f32[32,8192]{1,0:T(8,128)S(1)} fusion(s32[]{:T(128)} %get-tuple-element.189, s32[]{:T(128)} %bitcast.13, s32[8192]{0:T(1024)S(1)} %iota_multiply_fusion.2, s32[512]{0:T(512)S(1)} %add_multiply_fusion.2, f32[32,8192]{1,0:T(8,128)S(1)} %get-tuple-element.171, pred[]{:T(512)S(6)} %compare.3, ...), kind=kOutput, calls=%fused_computation.8.clone.1 | convolution fusion | flops 323485696 | bytes 2165765 | tf_op jit(solution)/shard_map/while/body/dot_general | solution.py:48
  84.9 12.7 %all-to-all-start = ((f32[32,32,256]{2,0,1:T(8,128)}), f32[32,32,256]{2,0,1:T(8,128)S(1)}, u32[]{:S(2)}, u32[]{:S(2)}) async-start(f32[32,32,256]{2,0,1:T(8,128)} %bitcast.11), calls=%async_computation | async-start | bytes 2097152 | tf_op jit(solution)/shard_map/all_to_all | solution.py:59
  97.7 28.5 %all-to-all-done = f32[32,32,256]{2,0,1:T(8,128)S(1)} async-done(((f32[32,32,256]{2,0,1:T(8,128)}), f32[32,32,256]{2,0,1:T(8,128)S(1)}, u32[]{:S(2)}, u32[]{:S(2)}) %all-to-all-start) | async-done | bytes 1048608 | tf_op jit(solution)/shard_map/all_to_all | solution.py:59
  126.2 19.0 %all_gather.3 = f32[512,256]{1,0:T(8,128)S(1)} all-gather(f32[32,256]{1,0:T(8,128)S(1)} %reduce_sum.27), channel_id=1, replica_groups=mesh['param'=32,'ex'=16] {'ex'}, dimensions={0}, use_global_device_ids=true | all-gather | bytes 557056 | tf_op jit(solution)/shard_map/all_gather | solution.py:61
  147.1 2.2 %collective-permute-start = (f32[8480]{0:T(1024)S(1)}, f32[8480]{0:T(1024)S(1)}, u32[]{:S(2)}, u32[]{:S(2)}) collective-permute-start(f32[8480]{0:T(1024)S(1)} %concatenate.3), channel_id=1, source_target_pairs={{0,16},{16,0},{32,48},{48,32},{64,80},{80,64},{96,112},{112,96},{1... | collective-permute-start | bytes 101768 | tf_op jit(solution)/shard_map/ppermute | solution.py:32
  149.3 3.6 %collective-permute-done = f32[8480]{0:T(1024)S(1)} collective-permute-done((f32[8480]{0:T(1024)S(1)}, f32[8480]{0:T(1024)S(1)}, u32[]{:S(2)}, u32[]{:S(2)}) %collective-permute-start) | collective-permute-done | bytes 33952 | tf_op jit(solution)/shard_map/ppermute | solution.py:32
  152.9 3.2 %collective-permute-start.1 = (f32[8480]{0:T(1024)S(1)}, f32[8480]{0:T(1024)S(1)}, u32[]{:S(2)}, u32[]{:S(2)}) collective-permute-start(f32[8480]{0:T(1024)S(1)} %add.91), channel_id=1, source_target_pairs={{0,32},{16,48},{32,0},{48,16},{64,96},{80,112},{96,64},{112,80},{1... | collective-permute-start | bytes 101768 | tf_op jit(solution)/shard_map/ppermute | solution.py:32
  156.1 3.5 %collective-permute-done.1 = f32[8480]{0:T(1024)S(1)} collective-permute-done((f32[8480]{0:T(1024)S(1)}, f32[8480]{0:T(1024)S(1)}, u32[]{:S(2)}, u32[]{:S(2)}) %collective-permute-start.1) | collective-permute-done | bytes 33952 | tf_op jit(solution)/shard_map/ppermute | solution.py:32
  159.7 2.5 %collective-permute-start.2 = (f32[8480]{0:T(1024)S(1)}, f32[8480]{0:T(1024)S(1)}, u32[]{:S(2)}, u32[]{:S(2)}) collective-permute-start(f32[8480]{0:T(1024)S(1)} %add.92), channel_id=1, source_target_pairs={{0,64},{16,80},{32,96},{48,112},{64,0},{80,16},{96,32},{112,48},{1... | collective-permute-start | bytes 101768 | tf_op jit(solution)/shard_map/ppermute | solution.py:32
  162.2 7.3 %collective-permute-done.2 = f32[8480]{0:T(1024)S(1)} collective-permute-done((f32[8480]{0:T(1024)S(1)}, f32[8480]{0:T(1024)S(1)}, u32[]{:S(2)}, u32[]{:S(2)}) %collective-permute-start.2) | collective-permute-done | bytes 33952 | tf_op jit(solution)/shard_map/ppermute | solution.py:32
  169.4 2.6 %collective-permute-start.3 = (f32[8480]{0:T(1024)S(1)}, f32[8480]{0:T(1024)S(1)}, u32[]{:S(2)}, u32[]{:S(2)}) collective-permute-start(f32[8480]{0:T(1024)S(1)} %add.93), channel_id=1, source_target_pairs={{0,128},{16,144},{32,160},{48,176},{64,192},{80,208},{96,224},{112... | collective-permute-start | bytes 101768 | tf_op jit(solution)/shard_map/ppermute | solution.py:32
  172.0 3.3 %collective-permute-done.3 = f32[8480]{0:T(1024)S(1)} collective-permute-done((f32[8480]{0:T(1024)S(1)}, f32[8480]{0:T(1024)S(1)}, u32[]{:S(2)}, u32[]{:S(2)}) %collective-permute-start.3) | collective-permute-done | bytes 33952 | tf_op jit(solution)/shard_map/ppermute | solution.py:32
  175.3 3.5 %collective-permute-start.4 = (f32[8480]{0:T(1024)S(1)}, f32[8480]{0:T(1024)S(1)}, u32[]{:S(2)}, u32[]{:S(2)}) collective-permute-start(f32[8480]{0:T(1024)S(1)} %add.94), channel_id=1, source_target_pairs={{0,256},{16,272},{32,288},{48,304},{64,320},{80,336},{96,352},{112... | collective-permute-start | bytes 101768 | tf_op jit(solution)/shard_map/ppermute | solution.py:32
  178.7 3.9 %collective-permute-done.4 = f32[8480]{0:T(1024)S(1)} collective-permute-done((f32[8480]{0:T(1024)S(1)}, f32[8480]{0:T(1024)S(1)}, u32[]{:S(2)}, u32[]{:S(2)}) %collective-permute-start.4) | collective-permute-done | bytes 33952 | tf_op jit(solution)/shard_map/ppermute | solution.py:32
  (47 shorter events, 12.6 us)
Async XLA Ops:
  84.9 12.7 %copy-start = (s32[256]{0:T(256)S(1)}, s32[256]{0:T(256)}, u32[]{:S(2)}) copy-start(s32[256]{0:T(256)} %param.7) | copy-start | bytes 3076
  84.9 41.2 %all-to-all-start = ((f32[32,32,256]{2,0,1:T(8,128)}), f32[32,32,256]{2,0,1:T(8,128)S(1)}, u32[]{:S(2)}, u32[]{:S(2)}) async-start(f32[32,32,256]{2,0,1:T(8,128)} %bitcast.11), calls=%async_computation | async-start | bytes 2097152 | tf_op jit(solution)/shard_map/all_to_all | solution.py:59
  147.1 5.8 %collective-permute-start = (f32[8480]{0:T(1024)S(1)}, f32[8480]{0:T(1024)S(1)}, u32[]{:S(2)}, u32[]{:S(2)}) collective-permute-start(f32[8480]{0:T(1024)S(1)} %concatenate.3), channel_id=1, source_target_pairs={{0,16},{16,0},{32,48},{48,32},{64,80},{80,64},{96,112},{112,96},{1... | collective-permute-start | bytes 101768 | tf_op jit(solution)/shard_map/ppermute | solution.py:32
  152.9 6.7 %collective-permute-start.1 = (f32[8480]{0:T(1024)S(1)}, f32[8480]{0:T(1024)S(1)}, u32[]{:S(2)}, u32[]{:S(2)}) collective-permute-start(f32[8480]{0:T(1024)S(1)} %add.91), channel_id=1, source_target_pairs={{0,32},{16,48},{32,0},{48,16},{64,96},{80,112},{96,64},{112,80},{1... | collective-permute-start | bytes 101768 | tf_op jit(solution)/shard_map/ppermute | solution.py:32
  159.7 9.7 %collective-permute-start.2 = (f32[8480]{0:T(1024)S(1)}, f32[8480]{0:T(1024)S(1)}, u32[]{:S(2)}, u32[]{:S(2)}) collective-permute-start(f32[8480]{0:T(1024)S(1)} %add.92), channel_id=1, source_target_pairs={{0,64},{16,80},{32,96},{48,112},{64,0},{80,16},{96,32},{112,48},{1... | collective-permute-start | bytes 101768 | tf_op jit(solution)/shard_map/ppermute | solution.py:32
  169.4 5.8 %collective-permute-start.3 = (f32[8480]{0:T(1024)S(1)}, f32[8480]{0:T(1024)S(1)}, u32[]{:S(2)}, u32[]{:S(2)}) collective-permute-start(f32[8480]{0:T(1024)S(1)} %add.93), channel_id=1, source_target_pairs={{0,128},{16,144},{32,160},{48,176},{64,192},{80,208},{96,224},{112... | collective-permute-start | bytes 101768 | tf_op jit(solution)/shard_map/ppermute | solution.py:32
  175.3 7.3 %collective-permute-start.4 = (f32[8480]{0:T(1024)S(1)}, f32[8480]{0:T(1024)S(1)}, u32[]{:S(2)}, u32[]{:S(2)}) collective-permute-start(f32[8480]{0:T(1024)S(1)} %add.94), channel_id=1, source_target_pairs={{0,256},{16,272},{32,288},{48,304},{64,320},{80,336},{96,352},{112... | collective-permute-start | bytes 101768 | tf_op jit(solution)/shard_map/ppermute | solution.py:32
